TPU v7x, 32 devices: a whole 2x2x4 slice. The times are simulated.
32 devices in a mesh: group: 2 (over x), dev: 16 (over z, y, core).
Axes of the slice: x: 2, y: 2, z: 4, core: 2. Of those that a mesh axis runs over, the one named last changes fastest.
Arguments:
- suffix_x: bfloat16 [2, 4096, 1600], P('group', 'dev'), may hold values from -6 to 6
- suffix_query: bfloat16 [2, 4096, 1024], P('group', 'dev'), may hold values from -128 to 128
- suffix_keyval: bfloat16 [2, 4096, 2048], P('group', 'dev'), may hold values from -6 to 6
- prefix_keyval: bfloat16 [2, 128, 2048], P('group', 'dev'), may hold values from -6 to 6
- prefix_hidden: bfloat16 [2, 128, 1600], P('group', 'dev'), may hold values from -6 to 6
- kv_weight: bfloat16 [1600, 2048], replicated, may hold values from -0.15625 to 0.15625
- out_weight: bfloat16 [1024, 1600], replicated, may hold values from -0.1875 to 0.1875
- fc_weight: bfloat16 [1600, 3840], P(None, ('group', 'dev')), may hold values from -0.15625 to 0.15625
- proj_weight: bfloat16 [3840, 1600], P(('group', 'dev')), may hold values from -0.09375 to 0.09375
- lengths: int32 [2, 16], P('group'), may hold values from 1 to 256, 2048 in all within a row
- placement: int32 [2, 16], P('group'), may hold values from 0 to 15, each once within a row
- owners: int32 [2, 16], P('group'), may hold values from 0 to 15, each once within a row
- recompute: int32 [2, 2], P('group'), may hold values from 0 to 15
Outputs:
- layer_out: bfloat16 [2, 4096, 1600], P('group', 'dev')
All inputs are finite; a program needn't handle non-finite values.
Results may differ from a plain program's by a relative error of at most 0.008.
Values may be sent and summed in bfloat16 or wider, within the bound.
No kernel may reach another device: no remote copies, remote signals or barrier semaphores. Data moves between devices by JAX's collectives and lax.ppermute only.
A program may use at most 128 MiB of HBM per device.

v0:
```python
import jax
import jax.numpy as jnp
from jax import lax
from jax.sharding import PartitionSpec as P

HEAD_DIM = 64
NEGATIVE = -1e30
EPSILON = 1e-05
SCORE_SCALE = 0.125


def normalize(values_in):
    values_in = values_in.astype(jnp.float32)
    average = jnp.mean(values_in, axis=-1, keepdims=True)
    centered = values_in - average
    variance = jnp.mean(centered * centered, axis=-1, keepdims=True)
    return centered / jnp.sqrt(variance + EPSILON)


def absorb(state, queries, keyval, allowed):
    running_top, running_total, accumulated = state
    head_count = queries.shape[1]
    head_size = queries.shape[2]
    row_count = keyval.shape[0]
    width_att = head_count * head_size
    key_rows = keyval[:, :width_att].reshape(row_count, head_count, head_size)
    val_rows = keyval[:, width_att:].reshape(row_count, head_count, head_size)
    scores = (
        jnp.einsum("qhd,khd->hqk", queries, key_rows, preferred_element_type=jnp.float32)
        * SCORE_SCALE
    )
    scores = jnp.where(allowed[None], scores, NEGATIVE)
    new_top = jnp.maximum(running_top, jnp.max(scores, axis=-1))
    factor = jnp.exp(running_top - new_top)
    weights = jnp.where(allowed[None], jnp.exp(scores - new_top[:, :, None]), 0.0)
    running_total = running_total * factor + jnp.sum(weights, axis=-1)
    weights_low = weights.astype(jnp.bfloat16)
    update = jnp.einsum("hqk,khd->qhd", weights_low, val_rows, preferred_element_type=jnp.float32)
    accumulated = accumulated * jnp.transpose(factor)[:, :, None] + update
    return (new_top, running_total, accumulated)


def per_device(
    suffix_x,
    suffix_query,
    suffix_keyval,
    prefix_keyval,
    prefix_hidden,
    kv_weight,
    out_weight,
    fc_weight,
    proj_weight,
    lengths,
    placement,
    owners,
    recompute,
):
    device_count = lax.axis_size("dev")
    my_device = lax.axis_index("dev")
    slots = suffix_x.shape[1]
    block_rows = prefix_keyval.shape[1]
    width_att = suffix_query.shape[2]
    head_count = width_att // HEAD_DIM
    device_ids = jnp.arange(device_count, dtype=jnp.int32)
    hits = placement[0][:, None] == device_ids[None, :]
    device_length = jnp.sum(jnp.where(hits, lengths[0][:, None], 0), axis=0)
    my_length = jnp.sum(jnp.where(device_ids == my_device, device_length, 0))
    block_ids = jnp.arange(owners.shape[1], dtype=jnp.int32)
    chosen = recompute[0]
    chosen_owner = jnp.sum(
        jnp.where(chosen[:, None] == block_ids[None, :], owners[0][None, :], 0), axis=1
    )
    stale_device = jnp.any(chosen_owner[:, None] == device_ids[None, :], axis=0)
    queries = suffix_query[0].reshape(slots, head_count, HEAD_DIM)
    normed_prefix = normalize(prefix_hidden[0]).astype(jnp.bfloat16)
    fresh = jnp.dot(normed_prefix, kv_weight, preferred_element_type=jnp.float32).astype(
        jnp.bfloat16
    )
    my_stale = jnp.any(chosen_owner == my_device)
    local_kv = jnp.where(my_stale, fresh, prefix_keyval[0])
    skip_device = jnp.zeros_like(stale_device)
    gathered = lax.all_gather(local_kv, "dev", axis=0, tiled=True)
    prefix_count = gathered.shape[0]
    row_device = jnp.arange(prefix_count, dtype=jnp.int32) // block_rows
    skipped = jnp.any((row_device[:, None] == device_ids[None, :]) & skip_device[None, :], axis=1)
    state = (
        jnp.full((head_count, slots), NEGATIVE, jnp.float32),
        jnp.zeros((head_count, slots), jnp.float32),
        jnp.zeros((slots, head_count, HEAD_DIM), jnp.float32),
    )
    key_block = 512 if prefix_count % 512 == 0 else prefix_count
    for block_start in range(0, prefix_count, key_block):
        kept = jnp.logical_not(skipped[block_start : block_start + key_block])
        allowed = jnp.broadcast_to(kept[None, :], (slots, key_block))
        state = absorb(state, queries, gathered[block_start : block_start + key_block], allowed)
    positions = jnp.arange(slots, dtype=jnp.int32)
    causal = (positions[None, :] <= positions[:, None]) & (positions[None, :] < my_length)
    state = absorb(state, queries, suffix_keyval[0], causal)
    final_top, final_total, accumulated = state
    attended = (
        (accumulated / jnp.transpose(final_total)[:, :, None])
        .reshape(slots, width_att)
        .astype(jnp.bfloat16)
    )
    projected = jnp.dot(attended, out_weight, preferred_element_type=jnp.float32)
    residual = suffix_x[0].astype(jnp.float32) + projected
    normed = normalize(residual).astype(jnp.bfloat16)
    fc_full, proj_full = (
        lax.all_gather(fc_weight, ("group", "dev"), axis=1, tiled=True),
        lax.all_gather(proj_weight, ("group", "dev"), axis=0, tiled=True),
    )
    inner = jnp.dot(normed, fc_full, preferred_element_type=jnp.float32)
    activated = jax.nn.gelu(inner, approximate=True).astype(jnp.bfloat16)
    feed_out = jnp.dot(activated, proj_full, preferred_element_type=jnp.float32)
    live = positions[:, None] < my_length
    return jnp.where(live, residual + feed_out, 0.0).astype(jnp.bfloat16)[None]


def solution(mesh):
    return jax.shard_map(
        per_device,
        mesh=mesh,
        in_specs=(
            P("group", "dev", None),
            P("group", "dev", None),
            P("group", "dev", None),
            P("group", "dev", None),
            P("group", "dev", None),
            P(),
            P(),
            P(None, ("group", "dev")),
            P(("group", "dev"), None),
            P("group", None),
            P("group", None),
            P("group", None),
            P("group", None),
        ),
        out_specs=P("group", "dev", None),
        check_vma=False,
    )
```

profile of v0, /device:TPU:0, one launch (start us, length us, event | category | flops | bytes accessed | tf_op | source)
XLA Modules:
  0.0 235.2 jit_solution(8602153443183435182)
XLA Ops:
  6.6 0.7 all-gather.3.cloned.1.call-update
  7.3 0.7 all-gather.5.cloned.1.call-update
  8.0 2.2 fusion.67
  10.3 2.0 copy.33
  12.3 2.1 copy.30
  14.6 0.6 compare_reduce_fusion
  15.6 4.5 %fusion.14 = bf16[8,2048]{1,0:T(8,128)(2,1)S(1)} fusion(bf16[1600,2048]{1,0:T(8,128)(2,1)} %param.18, bf16[1,8,2048]{2,1,0:T(8,128)(2,1)S(1)} %copy-done.5, pred[]{:T(512)} %compare_reduce_fusion, bf16[1,8,1600]{2,1,0:T(8,128)(2,1)S(1)} %copy-done.4, f32[8]{0:T(128)S(1)} %add_sqrt_fusion.1, f32[8]{0:T(128)S(1)} %broadcast_multiply_fusion.1), kind=kOutput, calls=%fused_computation.20 | convolution fusion | flops 52512768 | bytes 6644801 | tf_op jit(solution)/shard_map/dot_general | solution.py:76
  20.1 25.2 %all_gather.9 = bf16[128,2048]{1,0:T(8,128)(2,1)S(1)} all-gather(bf16[8,2048]{1,0:T(8,128)(2,1)S(1)} %fusion.14), channel_id=1, replica_groups=mesh['group'=2,'dev'=16] {'dev'}, dimensions={0}, use_global_device_ids=true | all-gather | bytes 557056 | tf_op jit(solution)/shard_map/all_gather | solution.py:82
  45.3 0.7 fusion.68
  46.1 1.8 copy.29
  47.9 2.0 copy.34
  49.9 0.8 copy.31
  50.8 0.6 fusion.56
  51.5 0.6 iota_compare_fusion.2
  52.2 1.6 bitcast_reduce_fusion
  53.9 2.0 fusion.8
  56.3 1.0 fusion.9
  57.3 1.1 fusion.26
  58.5 0.6 fusion.33
  59.6 1.1 fusion.69
  60.7 1.2 copy-done.1
  62.2 49.0 %all-gather.3.cloned.1.call-done = bf16[1600,3840]{0,1:T(8,128)(2,1)} async-done(((bf16[1600,120]{0,1:T(8,128)(2,1)}), bf16[1600,3840]{0,1:T(8,128)(2,1)}) %all-gather.3.cloned.1.call-update) | async-done | bytes 12288016 | tf_op jit(solution)/shard_map/all_gather | solution.py:109
  111.2 98.2 %all-gather.5.cloned.1.call-done = bf16[3840,1600]{1,0:T(8,128)(2,1)} async-done(((bf16[120,1600]{1,0:T(8,128)(2,1)}), bf16[3840,1600]{1,0:T(8,128)(2,1)}) %all-gather.5.cloned.1.call-update) | async-done | bytes 12288016 | tf_op jit(solution)/shard_map/all_gather | solution.py:110
  209.4 19.0 %fusion.13 = bf16[1,256,1600]{1,2,0:T(8,128)(2,1)} fusion(f32[256,1600]{0,1:T(8,128)} %copy-done.1, bf16[3840,1600]{1,0:T(8,128)(2,1)} %all-gather.5.cloned.1.call-done, bf16[1600,3840]{0,1:T(8,128)(2,1)} %all-gather.3.cloned.1.call-done, f32[256]{0:T(256)S(1)} %add_sqrt_fusion, f32[256]{0:T(256)S(1)} %broadcast_multiply_fusion, ...), kind=kOutput, calls=%fused_computation.18 | convolution fusion | flops 6302760960 | bytes 27035904 | tf_op jit(solution)/shard_map/dot_general | solution.py:114
  (36 shorter events, 2.0 us)
Async XLA Ops:
  6.5 52.6 %copy-start = (bf16[1024,1600]{0,1:T(8,128)(2,1)S(1)}, bf16[1024,1600]{0,1:T(8,128)(2,1)}, u32[]{:S(2)}) copy-start(bf16[1024,1600]{0,1:T(8,128)(2,1)} %param.19) | copy-start | bytes 9830404
  6.5 7.9 %copy-start.8 = (s32[1,2]{1,0:T(1,128)S(1)}, s32[1,2]{1,0:T(1,128)}, u32[]{:S(2)}) copy-start(s32[1,2]{1,0:T(1,128)} %param.25) | copy-start | bytes 28
  6.5 7.9 %copy-start.7 = (s32[1,16]{1,0:T(1,128)S(1)}, s32[1,16]{1,0:T(1,128)}, u32[]{:S(2)}) copy-start(s32[1,16]{1,0:T(1,128)} %param.24) | copy-start | bytes 196
  6.5 8.7 %copy-start.4 = (bf16[1,8,1600]{2,1,0:T(8,128)(2,1)S(1)}, bf16[1,8,1600]{2,1,0:T(8,128)(2,1)}, u32[]{:S(2)}) copy-start(bf16[1,8,1600]{2,1,0:T(8,128)(2,1)} %param.17) | copy-start | bytes 76804
  6.5 9.1 %copy-start.5 = (bf16[1,8,2048]{2,1,0:T(8,128)(2,1)S(1)}, bf16[1,8,2048]{2,1,0:T(8,128)(2,1)}, u32[]{:S(2)}) copy-start(bf16[1,8,2048]{2,1,0:T(8,128)(2,1)} %param.16) | copy-start | bytes 98308
  6.5 104.7 %all-gather.3.cloned.1.call-start = ((), (), s32[]{:S(2)}) async-start(), calls=%async_computation | async-start | bytes 13178880 | tf_op jit(solution)/shard_map/all_gather | solution.py:109
  7.3 202.1 %all-gather.5.cloned.1.call-start = ((), (), s32[]{:S(2)}) async-start(), calls=%async_computation.1 | async-start | bytes 13178880 | tf_op jit(solution)/shard_map/all_gather | solution.py:110
  15.6 35.2 %copy-start.9 = (s32[1,16]{1,0:T(1,128)S(1)}, s32[1,16]{1,0:T(1,128)}, u32[]{:S(2)}) copy-start(s32[1,16]{1,0:T(1,128)} %param.22) | copy-start | bytes 196
  15.6 35.1 %copy-start.10 = (s32[1,16]{1,0:T(1,128)S(1)}, s32[1,16]{1,0:T(1,128)}, u32[]{:S(2)}) copy-start(s32[1,16]{1,0:T(1,128)} %param.23) | copy-start | bytes 196
  55.9 1.4 copy-start.2
  57.3 1.1 copy-start.3
  58.5 1.2 copy-start.6
  60.7 1.2 copy-start.1
Sparse Core Ops, SparseCore 0:
  10.2 100.9 all-gather.2
  114.0 95.2 all-gather.4
where the time goes:
time: 236 us; the launch traced here: 235 us
  waiting for transfers between devices  149 us (63%)
  matrix products  29.9 us (13%)
  blocking collectives  25.2 us (11%)
  local copies, waits for them, and re-layouts  13.6 us (6%)
  between operations  13.6 us (6%)
  other arithmetic  4.28 us (2%)
    all_gather x1, waiting for transfers between devices, per_device(): lax.all_gather(proj_weight, ('group', 'dev'), axis=0, tiled=True)  98.2 us
    all_gather x1, waiting for transfers between devices, per_device(): lax.all_gather(fc_weight, ('group', 'dev'), axis=1, tiled=True)  49 us
    all_gather x1, blocking collectives, per_device(): gathered = lax.all_gather(local_kv, 'dev', axis=0, tiled=True)  25.2 us
    dot_general x1, matrix products, per_device(): feed_out = jnp.dot(activated, proj_full, preferred_element_type=jnp.float32)  19 us
    slice x3, local copies, waits for them, and re-layouts, absorb(): key_rows = keyval[:, :width_att].reshape(row_count, head_count, head_size)  6.07 us
  transfers between devices with their start and end apart: 2, of which 2 were waited for; matrix products, arithmetic and copies ran while one was open for 11% of the time, Pallas kernels for 0%

commit v1 on v0

--- a/solution.py
+++ b/solution.py
@@ -7,6 +7,20 @@
 NEGATIVE = -1e30
 EPSILON = 1e-05
 SCORE_SCALE = 0.125
+
+
+def fit_the_columns(body):
+    q_n = lax.axis_size("dev")
+    tmp = sorted(((u, (u + 1) % q_n) for u in range(q_n)))
+    odd = body
+    pool = [odd]
+    for tick in range(1, q_n):
+        odd = lax.ppermute(odd, "dev", tmp)
+        pool.insert(0, odd)
+    all_values = jnp.concatenate(pool, 0)
+    big = lax.axis_index("dev")
+    moved = big + 1
+    return jnp.roll(all_values, moved * body.shape[0], 0)
 
 
 def normalize(values_in):
@@ -79,7 +93,7 @@
     my_stale = jnp.any(chosen_owner == my_device)
     local_kv = jnp.where(my_stale, fresh, prefix_keyval[0])
     skip_device = jnp.zeros_like(stale_device)
-    gathered = lax.all_gather(local_kv, "dev", axis=0, tiled=True)
+    gathered = fit_the_columns(local_kv)
     prefix_count = gathered.shape[0]
     row_device = jnp.arange(prefix_count, dtype=jnp.int32) // block_rows
     skipped = jnp.any((row_device[:, None] == device_ids[None, :]) & skip_device[None, :], axis=1)

time: 236 us -> 239 us (1.013)
  blocking collectives: 25.2 us -> 0 us
  local copies, waits for them, and re-layouts: 13.6 us -> 29.7 us
  waiting for transfers between devices: 149 us -> 154 us
    ppermute x0 -> x15, waiting for transfers between devices: none -> 86 us  [fit_the_columns(): odd = lax.ppermute(odd, 'dev', tmp)]
    all_gather x1, waiting for transfers between devices: 49 us -> 0.01 us  [per_device(): lax.all_gather(fc_weight, ('group', 'dev'), axis=1, tiled=True)]
    all_gather x1, waiting for transfers between devices: 98.2 us -> 66.5 us  [per_device(): lax.all_gather(proj_weight, ('group', 'dev'), axis=0, tiled=True)]
    all_gather x1 -> x0, blocking collectives: 25.2 us -> none  [per_device(): gathered = lax.all_gather(local_kv, 'dev', axis=0, tiled=True)]
    unnamed x23 -> x72, local copies, waits for them, and re-layouts: 3.87 us -> 21.2 us
  transfers between devices with their start and end apart: 2 -> 17, of which waited for: 2 -> 16; matrix products, arithmetic and copies ran while one was open for 11% -> 19% of each run, Pallas kernels for 0% -> 0%
where the time goes in v1:
time: 239 us; the launch traced here: 237 us
  waiting for transfers between devices  154 us (64%)
  matrix products  32.2 us (13%)
  local copies, waits for them, and re-layouts  29.7 us (12%)
  between operations  13.7 us (6%)
  other arithmetic  6.55 us (3%)
    ppermute x15, waiting for transfers between devices, fit_the_columns(): odd = lax.ppermute(odd, 'dev', tmp)  86 us
    all_gather x1, waiting for transfers between devices, per_device(): lax.all_gather(proj_weight, ('group', 'dev'), axis=0, tiled=True)  66.5 us
    unnamed x72, local copies, waits for them, and re-layouts  21.2 us
    dot_general x1, matrix products, per_device(): feed_out = jnp.dot(activated, proj_full, preferred_element_type=jnp.float32)  19.1 us
    dot_general x2, matrix products, absorb(): jnp.einsum('qhd,khd->hqk', queries, key_rows, preferred_element_type=jnp....  5.79 us
    slice x3, local copies, waits for them, and re-layouts, absorb(): key_rows = keyval[:, :width_att].reshape(row_count, head_count, head_size)  4.9 us
  transfers between devices with their start and end apart: 17, of which 16 were waited for; matrix products, arithmetic and copies ran while one was open for 19% of the time, Pallas kernels for 0%

profile of v1, /device:TPU:0, one launch (start us, length us, event | category | flops | bytes accessed | tf_op | source)
XLA Modules:
  0.0 236.7 jit_solution(15565037317143698968)
XLA Ops:
  11.4 4.5 %fusion.14 = bf16[8,2048]{1,0:T(8,128)(2,1)S(1)} fusion(bf16[1600,2048]{1,0:T(8,128)(2,1)} %param.18, bf16[1,8,2048]{2,1,0:T(8,128)(2,1)} %param.16, pred[]{:T(512)} %compare_reduce_fusion, bf16[1,8,1600]{2,1,0:T(8,128)(2,1)} %param.17, f32[8]{0:T(128)S(1)} %add_sqrt_fusion.1, f32[8]{0:T(128)S(1)} %broadcast_multiply_fusion.1), kind=kOutput, calls=%fused_computation.20 | convolution fusion | flops 52512768 | bytes 6644801 | tf_op jit(solution)/shard_map/dot_general | solution.py:90
  16.4 6.6 %collective-permute-done = bf16[8,2048]{1,0:T(8,128)(2,1)S(1)} collective-permute-done((bf16[8,2048]{1,0:T(8,128)(2,1)S(1)}, bf16[8,2048]{1,0:T(8,128)(2,1)S(1)}, u32[]{:S(2)}, u32[]{:S(2)}) %collective-permute-start) | collective-permute-done | bytes 32800 | tf_op jit(solution)/shard_map/ppermute | solution.py:18
  23.0 6.5 %collective-permute-done.1 = bf16[8,2048]{1,0:T(8,128)(2,1)S(1)} collective-permute-done((bf16[8,2048]{1,0:T(8,128)(2,1)S(1)}, bf16[8,2048]{1,0:T(8,128)(2,1)S(1)}, u32[]{:S(2)}, u32[]{:S(2)}) %collective-permute-start.1) | collective-permute-done | bytes 32800 | tf_op jit(solution)/shard_map/ppermute | solution.py:18
  29.6 6.6 %collective-permute-done.2 = bf16[8,2048]{1,0:T(8,128)(2,1)S(1)} collective-permute-done((bf16[8,2048]{1,0:T(8,128)(2,1)S(1)}, bf16[8,2048]{1,0:T(8,128)(2,1)S(1)}, u32[]{:S(2)}, u32[]{:S(2)}) %collective-permute-start.2) | collective-permute-done | bytes 32800 | tf_op jit(solution)/shard_map/ppermute | solution.py:18
  36.1 6.0 %collective-permute-done.3 = bf16[8,2048]{1,0:T(8,128)(2,1)S(1)} collective-permute-done((bf16[8,2048]{1,0:T(8,128)(2,1)S(1)}, bf16[8,2048]{1,0:T(8,128)(2,1)S(1)}, u32[]{:S(2)}, u32[]{:S(2)}) %collective-permute-start.3) | collective-permute-done | bytes 32800 | tf_op jit(solution)/shard_map/ppermute | solution.py:18
  42.2 6.8 %collective-permute-done.4 = bf16[8,2048]{1,0:T(8,128)(2,1)S(1)} collective-permute-done((bf16[8,2048]{1,0:T(8,128)(2,1)S(1)}, bf16[8,2048]{1,0:T(8,128)(2,1)S(1)}, u32[]{:S(2)}, u32[]{:S(2)}) %collective-permute-start.4) | collective-permute-done | bytes 32800 | tf_op jit(solution)/shard_map/ppermute | solution.py:18
  48.9 6.7 %collective-permute-done.5 = bf16[8,2048]{1,0:T(8,128)(2,1)S(1)} collective-permute-done((bf16[8,2048]{1,0:T(8,128)(2,1)S(1)}, bf16[8,2048]{1,0:T(8,128)(2,1)S(1)}, u32[]{:S(2)}, u32[]{:S(2)}) %collective-permute-start.5) | collective-permute-done | bytes 32800 | tf_op jit(solution)/shard_map/ppermute | solution.py:18
  56.2 6.6 %collective-permute-done.6 = bf16[8,2048]{1,0:T(8,128)(2,1)S(1)} collective-permute-done((bf16[8,2048]{1,0:T(8,128)(2,1)S(1)}, bf16[8,2048]{1,0:T(8,128)(2,1)S(1)}, u32[]{:S(2)}, u32[]{:S(2)}) %collective-permute-start.6) | collective-permute-done | bytes 32800 | tf_op jit(solution)/shard_map/ppermute | solution.py:18
  63.4 6.0 %collective-permute-done.7 = bf16[8,2048]{1,0:T(8,128)(2,1)S(1)} collective-permute-done((bf16[8,2048]{1,0:T(8,128)(2,1)S(1)}, bf16[8,2048]{1,0:T(8,128)(2,1)S(1)}, u32[]{:S(2)}, u32[]{:S(2)}) %collective-permute-start.7) | collective-permute-done | bytes 32800 | tf_op jit(solution)/shard_map/ppermute | solution.py:18
  70.1 6.7 %collective-permute-done.8 = bf16[8,2048]{1,0:T(8,128)(2,1)S(1)} collective-permute-done((bf16[8,2048]{1,0:T(8,128)(2,1)S(1)}, bf16[8,2048]{1,0:T(8,128)(2,1)S(1)}, u32[]{:S(2)}, u32[]{:S(2)}) %collective-permute-start.8) | collective-permute-done | bytes 32800 | tf_op jit(solution)/shard_map/ppermute | solution.py:18
  77.9 5.6 %collective-permute-done.9 = bf16[8,2048]{1,0:T(8,128)(2,1)S(1)} collective-permute-done((bf16[8,2048]{1,0:T(8,128)(2,1)S(1)}, bf16[8,2048]{1,0:T(8,128)(2,1)S(1)}, u32[]{:S(2)}, u32[]{:S(2)}) %collective-permute-start.9) | collective-permute-done | bytes 32800 | tf_op jit(solution)/shard_map/ppermute | solution.py:18
  83.6 6.6 %collective-permute-done.10 = bf16[8,2048]{1,0:T(8,128)(2,1)S(1)} collective-permute-done((bf16[8,2048]{1,0:T(8,128)(2,1)S(1)}, bf16[8,2048]{1,0:T(8,128)(2,1)S(1)}, u32[]{:S(2)}, u32[]{:S(2)}) %collective-permute-start.10) | collective-permute-done | bytes 32800 | tf_op jit(solution)/shard_map/ppermute | solution.py:18
  90.9 6.0 %collective-permute-done.11 = bf16[8,2048]{1,0:T(8,128)(2,1)S(1)} collective-permute-done((bf16[8,2048]{1,0:T(8,128)(2,1)S(1)}, bf16[8,2048]{1,0:T(8,128)(2,1)S(1)}, u32[]{:S(2)}, u32[]{:S(2)}) %collective-permute-start.11) | collective-permute-done | bytes 32800 | tf_op jit(solution)/shard_map/ppermute | solution.py:18
  97.6 6.2 %collective-permute-done.12 = bf16[8,2048]{1,0:T(8,128)(2,1)} collective-permute-done((bf16[8,2048]{1,0:T(8,128)(2,1)S(1)}, bf16[8,2048]{1,0:T(8,128)(2,1)}, u32[]{:S(2)}, u32[]{:S(2)}) %collective-permute-start.12) | collective-permute-done | bytes 32800 | tf_op jit(solution)/shard_map/ppermute | solution.py:18
  104.0 2.1 copy.30
  106.1 2.0 copy.33
  108.1 2.7 %collective-permute-done.13 = bf16[8,2048]{1,0:T(8,128)(2,1)} collective-permute-done((bf16[8,2048]{1,0:T(8,128)(2,1)}, bf16[8,2048]{1,0:T(8,128)(2,1)}, u32[]{:S(2)}, u32[]{:S(2)}) %collective-permute-start.13) | collective-permute-done | bytes 32800 | tf_op jit(solution)/shard_map/ppermute | solution.py:18
  110.8 4.0 %fusion.8 = (f32[16,256]{1,0:T(8,128)S(1)}, f32[16,256,256]{1,2,0:T(8,128)}) fusion(pred[256,256]{0,1:T(8,128)(4,1)S(1)} %fusion.42, bf16[256,16,64]{0,2,1:T(8,128)(2,1)} %bitcast.87, bf16[256,16,64]{0,2,1:T(8,128)(2,1)} %bitcast.89), kind=kOutput, calls=%fused_computation.11 | convolution fusion | flops 137359360 | bytes 5324800 | tf_op jit(solution)/shard_map/qhd,khd->hqk/dot_general | solution.py:43
  114.9 2.0 copy.34
  133.3 1.8 copy.29
  135.9 1.8 bitcast_reduce_fusion
  142.7 1.2 copy-done.2
  144.2 66.5 %all-gather.5.cloned.1.call-done = bf16[3840,1600]{1,0:T(8,128)(2,1)} async-done(((bf16[120,1600]{1,0:T(8,128)(2,1)}), bf16[3840,1600]{1,0:T(8,128)(2,1)}) %all-gather.5.cloned.1.call-update) | async-done | bytes 12288016 | tf_op jit(solution)/shard_map/all_gather | solution.py:124
  210.7 19.1 %fusion.13 = bf16[1,256,1600]{1,2,0:T(8,128)(2,1)} fusion(f32[256,1600]{0,1:T(8,128)} %copy-done.2, bf16[3840,1600]{1,0:T(8,128)(2,1)} %all-gather.5.cloned.1.call-done, bf16[1600,3840]{0,1:T(8,128)(2,1)} %all-gather.3.cloned.1.call-done, f32[256]{0:T(256)S(1)} %add_sqrt_fusion, f32[256]{0:T(256)S(1)} %broadcast_multiply_fusion, ...), kind=kOutput, calls=%fused_computation.18 | convolution fusion | flops 6302760960 | bytes 27035904 | tf_op jit(solution)/shard_map/dot_general | solution.py:128
  (115 shorter events, 32.1 us)
Async XLA Ops:
  6.5 134.6 %copy-start = (bf16[1024,1600]{0,1:T(8,128)(2,1)S(1)}, bf16[1024,1600]{0,1:T(8,128)(2,1)}, u32[]{:S(2)}) copy-start(bf16[1024,1600]{0,1:T(8,128)(2,1)} %param.19) | copy-start | bytes 9830404
  6.5 137.7 %all-gather.3.cloned.1.call-start = ((), (), s32[]{:S(2)}) async-start(), calls=%async_computation | async-start | bytes 13178880 | tf_op jit(solution)/shard_map/all_gather | solution.py:123
  7.3 203.5 %all-gather.5.cloned.1.call-start = ((), (), s32[]{:S(2)}) async-start(), calls=%async_computation.1 | async-start | bytes 13178880 | tf_op jit(solution)/shard_map/all_gather | solution.py:124
  8.0 68.8 %copy-start.3 = (bf16[1,256,2048]{2,1,0:T(8,128)(2,1)S(1)}, bf16[1,256,2048]{2,1,0:T(8,128)(2,1)}, u32[]{:S(2)}) copy-start(bf16[1,256,2048]{2,1,0:T(8,128)(2,1)} %param.15) | copy-start | bytes 3145732
  11.4 72.1 %copy-start.18 = (s32[1,16]{1,0:T(1,128)S(1)}, s32[1,16]{1,0:T(1,128)}, u32[]{:S(2)}) copy-start(s32[1,16]{1,0:T(1,128)} %param.22) | copy-start | bytes 196
  11.4 72.1 %copy-start.19 = (s32[1,16]{1,0:T(1,128)S(1)}, s32[1,16]{1,0:T(1,128)}, u32[]{:S(2)}) copy-start(s32[1,16]{1,0:T(1,128)} %param.23) | copy-start | bytes 196
  16.0 7.0 %collective-permute-start = (bf16[8,2048]{1,0:T(8,128)(2,1)S(1)}, bf16[8,2048]{1,0:T(8,128)(2,1)S(1)}, u32[]{:S(2)}, u32[]{:S(2)}) collective-permute-start(bf16[8,2048]{1,0:T(8,128)(2,1)S(1)} %fusion.14), channel_id=1, source_target_pairs={{0,1},{1,2},{2,3},{3,4},{4,5},{5,6},{6,7},{7,8},{8,9},{9,10},{10,1... | collective-permute-start | bytes 98312 | tf_op jit(solution)/shard_map/ppermute | solution.py:18
  23.0 6.5 %collective-permute-start.1 = (bf16[8,2048]{1,0:T(8,128)(2,1)S(1)}, bf16[8,2048]{1,0:T(8,128)(2,1)S(1)}, u32[]{:S(2)}, u32[]{:S(2)}) collective-permute-start(bf16[8,2048]{1,0:T(8,128)(2,1)S(1)} %collective-permute-done), channel_id=1, source_target_pairs={{0,1},{1,2},{2,3},{3,4},{4,5},{5,6},{6,7},{7,8},{8,9},{9,10},{10,1... | collective-permute-start | bytes 98312 | tf_op jit(solution)/shard_map/ppermute | solution.py:18
  29.6 6.6 %collective-permute-start.2 = (bf16[8,2048]{1,0:T(8,128)(2,1)S(1)}, bf16[8,2048]{1,0:T(8,128)(2,1)S(1)}, u32[]{:S(2)}, u32[]{:S(2)}) collective-permute-start(bf16[8,2048]{1,0:T(8,128)(2,1)S(1)} %collective-permute-done.1), channel_id=1, source_target_pairs={{0,1},{1,2},{2,3},{3,4},{4,5},{5,6},{6,7},{7,8},{8,9},{9,10},{10,1... | collective-permute-start | bytes 98312 | tf_op jit(solution)/shard_map/ppermute | solution.py:18
  36.1 6.0 %collective-permute-start.3 = (bf16[8,2048]{1,0:T(8,128)(2,1)S(1)}, bf16[8,2048]{1,0:T(8,128)(2,1)S(1)}, u32[]{:S(2)}, u32[]{:S(2)}) collective-permute-start(bf16[8,2048]{1,0:T(8,128)(2,1)S(1)} %collective-permute-done.2), channel_id=1, source_target_pairs={{0,1},{1,2},{2,3},{3,4},{4,5},{5,6},{6,7},{7,8},{8,9},{9,10},{10,1... | collective-permute-start | bytes 98312 | tf_op jit(solution)/shard_map/ppermute | solution.py:18
  42.2 6.8 %collective-permute-start.4 = (bf16[8,2048]{1,0:T(8,128)(2,1)S(1)}, bf16[8,2048]{1,0:T(8,128)(2,1)S(1)}, u32[]{:S(2)}, u32[]{:S(2)}) collective-permute-start(bf16[8,2048]{1,0:T(8,128)(2,1)S(1)} %collective-permute-done.3), channel_id=1, source_target_pairs={{0,1},{1,2},{2,3},{3,4},{4,5},{5,6},{6,7},{7,8},{8,9},{9,10},{10,1... | collective-permute-start | bytes 98312 | tf_op jit(solution)/shard_map/ppermute | solution.py:18
  48.9 6.7 %collective-permute-start.5 = (bf16[8,2048]{1,0:T(8,128)(2,1)S(1)}, bf16[8,2048]{1,0:T(8,128)(2,1)S(1)}, u32[]{:S(2)}, u32[]{:S(2)}) collective-permute-start(bf16[8,2048]{1,0:T(8,128)(2,1)S(1)} %collective-permute-done.4), channel_id=1, source_target_pairs={{0,1},{1,2},{2,3},{3,4},{4,5},{5,6},{6,7},{7,8},{8,9},{9,10},{10,1... | collective-permute-start | bytes 98312 | tf_op jit(solution)/shard_map/ppermute | solution.py:18
  56.2 6.6 %collective-permute-start.6 = (bf16[8,2048]{1,0:T(8,128)(2,1)S(1)}, bf16[8,2048]{1,0:T(8,128)(2,1)S(1)}, u32[]{:S(2)}, u32[]{:S(2)}) collective-permute-start(bf16[8,2048]{1,0:T(8,128)(2,1)S(1)} %collective-permute-done.5), channel_id=1, source_target_pairs={{0,1},{1,2},{2,3},{3,4},{4,5},{5,6},{6,7},{7,8},{8,9},{9,10},{10,1... | collective-permute-start | bytes 98312 | tf_op jit(solution)/shard_map/ppermute | solution.py:18
  63.4 6.0 %collective-permute-start.7 = (bf16[8,2048]{1,0:T(8,128)(2,1)S(1)}, bf16[8,2048]{1,0:T(8,128)(2,1)S(1)}, u32[]{:S(2)}, u32[]{:S(2)}) collective-permute-start(bf16[8,2048]{1,0:T(8,128)(2,1)S(1)} %collective-permute-done.6), channel_id=1, source_target_pairs={{0,1},{1,2},{2,3},{3,4},{4,5},{5,6},{6,7},{7,8},{8,9},{9,10},{10,1... | collective-permute-start | bytes 98312 | tf_op jit(solution)/shard_map/ppermute | solution.py:18
  70.1 6.7 %collective-permute-start.8 = (bf16[8,2048]{1,0:T(8,128)(2,1)S(1)}, bf16[8,2048]{1,0:T(8,128)(2,1)S(1)}, u32[]{:S(2)}, u32[]{:S(2)}) collective-permute-start(bf16[8,2048]{1,0:T(8,128)(2,1)S(1)} %collective-permute-done.7), channel_id=1, source_target_pairs={{0,1},{1,2},{2,3},{3,4},{4,5},{5,6},{6,7},{7,8},{8,9},{9,10},{10,1... | collective-permute-start | bytes 98312 | tf_op jit(solution)/shard_map/ppermute | solution.py:18
  76.8 27.0 %copy-start.11 = (bf16[8,2048]{1,0:T(8,128)(2,1)}, bf16[8,2048]{1,0:T(8,128)(2,1)S(1)}, u32[]{:S(2)}) copy-start(bf16[8,2048]{1,0:T(8,128)(2,1)S(1)} %collective-permute-done.8) | copy-start | bytes 98308
  76.8 6.7 %collective-permute-start.9 = (bf16[8,2048]{1,0:T(8,128)(2,1)S(1)}, bf16[8,2048]{1,0:T(8,128)(2,1)S(1)}, u32[]{:S(2)}, u32[]{:S(2)}) collective-permute-start(bf16[8,2048]{1,0:T(8,128)(2,1)S(1)} %collective-permute-done.8), channel_id=1, source_target_pairs={{0,1},{1,2},{2,3},{3,4},{4,5},{5,6},{6,7},{7,8},{8,9},{9,10},{10,1... | collective-permute-start | bytes 98312 | tf_op jit(solution)/shard_map/ppermute | solution.py:18
  83.5 20.3 %copy-start.12 = (bf16[8,2048]{1,0:T(8,128)(2,1)}, bf16[8,2048]{1,0:T(8,128)(2,1)S(1)}, u32[]{:S(2)}) copy-start(bf16[8,2048]{1,0:T(8,128)(2,1)S(1)} %collective-permute-done.9) | copy-start | bytes 98308
  83.5 6.7 %collective-permute-start.10 = (bf16[8,2048]{1,0:T(8,128)(2,1)S(1)}, bf16[8,2048]{1,0:T(8,128)(2,1)S(1)}, u32[]{:S(2)}, u32[]{:S(2)}) collective-permute-start(bf16[8,2048]{1,0:T(8,128)(2,1)S(1)} %collective-permute-done.9), channel_id=1, source_target_pairs={{0,1},{1,2},{2,3},{3,4},{4,5},{5,6},{6,7},{7,8},{8,9},{9,10},{10,1... | collective-permute-start | bytes 98312 | tf_op jit(solution)/shard_map/ppermute | solution.py:18
  90.2 6.7 %collective-permute-start.11 = (bf16[8,2048]{1,0:T(8,128)(2,1)S(1)}, bf16[8,2048]{1,0:T(8,128)(2,1)S(1)}, u32[]{:S(2)}, u32[]{:S(2)}) collective-permute-start(bf16[8,2048]{1,0:T(8,128)(2,1)S(1)} %collective-permute-done.10), channel_id=1, source_target_pairs={{0,1},{1,2},{2,3},{3,4},{4,5},{5,6},{6,7},{7,8},{8,9},{9,10},{10,1... | collective-permute-start | bytes 98312 | tf_op jit(solution)/shard_map/ppermute | solution.py:18
  96.9 6.9 %collective-permute-start.12 = (bf16[8,2048]{1,0:T(8,128)(2,1)S(1)}, bf16[8,2048]{1,0:T(8,128)(2,1)}, u32[]{:S(2)}, u32[]{:S(2)}) collective-permute-start(bf16[8,2048]{1,0:T(8,128)(2,1)S(1)} %collective-permute-done.11), channel_id=1, source_target_pairs={{0,1},{1,2},{2,3},{3,4},{4,5},{5,6},{6,7},{7,8},{8,9},{9,10},{10,1... | collective-permute-start | bytes 98312 | tf_op jit(solution)/shard_map/ppermute | solution.py:18
  103.8 7.0 %collective-permute-start.13 = (bf16[8,2048]{1,0:T(8,128)(2,1)}, bf16[8,2048]{1,0:T(8,128)(2,1)}, u32[]{:S(2)}, u32[]{:S(2)}) collective-permute-start(bf16[8,2048]{1,0:T(8,128)(2,1)} %collective-permute-done.12), channel_id=1, source_target_pairs={{0,1},{1,2},{2,3},{3,4},{4,5},{5,6},{6,7},{7,8},{8,9},{9,10},{10,1... | collective-permute-start | bytes 98312 | tf_op jit(solution)/shard_map/ppermute | solution.py:18
  110.8 6.4 %collective-permute-start.14 = (bf16[8,2048]{1,0:T(8,128)(2,1)}, bf16[8,2048]{1,0:T(8,128)(2,1)}, u32[]{:S(2)}, u32[]{:S(2)}) collective-permute-start(bf16[8,2048]{1,0:T(8,128)(2,1)} %collective-permute-done.13), channel_id=1, source_target_pairs={{0,1},{1,2},{2,3},{3,4},{4,5},{5,6},{6,7},{7,8},{8,9},{9,10},{10,1... | collective-permute-start | bytes 98312 | tf_op jit(solution)/shard_map/ppermute | solution.py:18
  141.7 69.1 %copy-start.16 = (pred[256]{0:T(512)(128)(4,1)S(1)}, pred[256]{0:T(512)(128)(4,1)}, u32[]{:S(2)}) copy-start(pred[256]{0:T(512)(128)(4,1)} %copy-done.15) | copy-start | bytes 772
  (13 other events, 51.6 us)
Sparse Core Ops, SparseCore 0:
  10.2 101.5 all-gather.2
  114.7 96.0 all-gather.4
